TPU v7x, 32 devices: a whole 2x2x4 slice. The times are simulated.
32 devices in a mesh: tok: 4 (over y, x), voc: 8 (over z, core).
Axes of the slice: x: 2, y: 2, z: 4, core: 2. Of those that a mesh axis runs over, the one named last changes fastest.
Arguments:
- hidden: bfloat16 [8192, 2048], P(('tok', 'voc')), as said below
- gain: bfloat16 [2048], replicated, may hold values from 0.5 to 1.5
- head: bfloat16 [2048, 50304], P(None, 'voc')
- targets: int32 [8192], replicated, may hold values from 0 to 50303
- lengths: int32 [8], replicated, may hold values from 1 to 1024, 5120 in all
- perm: int32 [8], replicated, may hold values from 0 to 7, each once
Outputs:
- logprob: float32 [5120], P(('tok', 'voc'))
- entropy: float32 [5120], P(('tok', 'voc'))
Inputs may be any that keep to these rules, and one draw needn't show every extreme that they name: Each request has at least one token and the longest has exactly 1024; the lengths sum to 5120. `perm`: each request is held by exactly one slot. `hidden`: rows past a request's length in its slot are not read by any output.
All inputs are finite; a program needn't handle non-finite values.
Results may differ from a plain program's by a relative error of at most 0.0024.
Values may be sent and summed in bfloat16 or wider, within the bound.
No kernel may reach another device: no remote copies, remote signals or barrier semaphores. Data moves between devices by JAX's collectives and lax.ppermute only.
A program may use at most 256 MiB of HBM per device.

v0:
```python
import jax
import jax.numpy as jnp
from jax import lax
from jax.sharding import PartitionSpec as P

MAXLEN = 1024


def slot_rows(positions, lengths, perm):
    count = lengths.shape[0]
    ident = jnp.arange(count, dtype=jnp.int32)
    starts = jnp.cumsum(lengths) - lengths
    request = jnp.sum((positions[:, None] >= starts[None, :]).astype(jnp.int32), axis=1) - 1
    start_of = jnp.sum(jnp.where(ident[None, :] == request[:, None], starts[None, :], 0), axis=1)
    slot_of = jnp.sum(jnp.where(perm[None, :] == request[:, None], ident[None, :], 0), axis=1)
    return slot_of * MAXLEN + positions - start_of


def row_stats(piece, weights, wanted):
    logits = jnp.dot(piece, weights, preferred_element_type=jnp.float32)
    top = jnp.max(logits, axis=1)
    expo = jnp.exp(logits - top[:, None])
    total = jnp.sum(expo, axis=1)
    moment = jnp.sum(expo * logits, axis=1)
    columns = jnp.arange(logits.shape[1], dtype=jnp.int32)
    picked = jnp.sum(jnp.where(columns[None, :] == wanted[:, None], logits, 0.0), axis=1)
    return jnp.stack([top, total, moment, picked], axis=0)


def make_stats(weights, col_base, row_base, targets, slot_len):
    count = slot_len.shape[0]
    ident = jnp.arange(count, dtype=jnp.int32)

    def compute(piece, start):
        size = piece.shape[0]
        rows = row_base + jnp.arange(size, dtype=jnp.int32)
        slot = rows // MAXLEN
        row_len = jnp.sum(jnp.where(slot[:, None] == ident[None, :], slot_len[None, :], 0), axis=1)
        live = rows % MAXLEN < row_len
        wanted = lax.dynamic_slice_in_dim(targets, row_base, size, 0) - col_base

        def busy(operand):
            return row_stats(piece, weights, wanted)

        def quiet(operand):
            zeros = jnp.zeros((size,), jnp.float32)
            return jnp.stack([zeros, zeros + 1.0, zeros, zeros], axis=0)

        return lax.cond(jnp.any(live), busy, quiet, 0)

    return compute


def finish(top, total, moment, picked):
    lse = top + jnp.log(total)
    return (picked - lse, lse - moment / total)


def on_device(hidden, gain, head, targets, lengths, perm):
    values = hidden.astype(jnp.float32)
    scale = lax.rsqrt(jnp.mean(values * values, axis=1, keepdims=True) + 1e-06)
    normed = (values * scale * gain.astype(jnp.float32)[None, :]).astype(jnp.bfloat16)
    count = lengths.shape[0]
    ident = jnp.arange(count, dtype=jnp.int32)
    slot_len = jnp.sum(jnp.where(perm[:, None] == ident[None, :], lengths[None, :], 0), axis=1)
    n_tok = lax.axis_size("tok")
    n_voc = lax.axis_size("voc")
    shard_cols = head.shape[1]
    voc_index = lax.axis_index("voc")
    tok_index = lax.axis_index("tok")
    out_rows = count * MAXLEN * 5 // 8 // (n_tok * n_voc)
    device = lax.axis_index(("tok", "voc"))
    group_rows = normed.shape[0] * n_voc
    compute = make_stats(head, voc_index * shard_cols, tok_index * group_rows, targets, slot_len)
    stats = compute(lax.all_gather(normed, "voc", axis=0, tiled=True), jnp.int32(0))
    top = lax.pmax(stats[0], "voc")
    factor = jnp.exp(stats[0] - top)
    total, moment, picked = lax.psum((stats[1] * factor, stats[2] * factor, stats[3]), "voc")
    own_lp, own_ent = finish(top, total, moment, picked)
    row_logprob, row_entropy = (
        lax.all_gather(own_lp, "tok", axis=0, tiled=True),
        lax.all_gather(own_ent, "tok", axis=0, tiled=True),
    )
    positions = device * out_rows + jnp.arange(out_rows, dtype=jnp.int32)
    rows = slot_rows(positions, lengths, perm)
    return (row_logprob[rows], row_entropy[rows])


def solution(mesh):
    in_specs = (P(("tok", "voc"), None), P(), P(None, "voc"), P(), P(), P())
    out_specs = (P(("tok", "voc")), P(("tok", "voc")))
    return jax.shard_map(
        on_device, mesh=mesh, in_specs=in_specs, out_specs=out_specs, check_vma=False
    )
```

profile of v0, /device:TPU:0, one launch (start us, length us, event | category | flops | bytes accessed | tf_op | source)
XLA Modules:
  0.0 252.4 jit_solution(14086592134587553559)
XLA Ops:
  7.2 0.0 all-gather.2.cloned.1.call-start
  7.2 0.7 convert_element_type.17
  7.9 1.5 fusion.1
  9.4 2.5 %fusion.3 = bf16[256,2048]{1,0:T(8,128)(2,1)} fusion(bf16[256,2048]{1,0:T(8,128)(2,1)} %param.8, f32[2048]{0:T(1024)S(1)} %convert_element_type.17, f32[256]{0:T(256)S(1)} %add_rsqrt_fusion), kind=kLoop, calls=%fused_computation.13 | loop fusion | flops 2097152 | bytes 2106368 | tf_op jit(solution)/shard_map/convert_element_type | solution.py:62
  11.9 0.0 all-gather.2.cloned.1.call-update
  12.0 0.9 select_reduce_fusion.4
  12.9 0.1 select_reduce_fusion.1
  12.9 0.6 fusion.10
  14.2 0.8 reduce-window.9
  15.1 0.7 bitcast_subtract_fusion
  15.7 0.1 convert_reduce_fusion
  15.8 0.7 select_reduce_fusion.3
  16.6 80.3 %all-gather.2.cloned.1.call-done = bf16[2048,2048]{1,0:T(8,128)(2,1)} async-done(((bf16[256,2048]{1,0:T(8,128)(2,1)}), bf16[2048,2048]{1,0:T(8,128)(2,1)}) %all-gather.2.cloned.1.call-update) | async-done | bytes 8388624 | tf_op jit(solution)/shard_map/all_gather | solution.py:75
  96.9 87.8 %conditional.1 = (f32[4,2048]{1,0:T(4,128)S(1)}) conditional(s32[]{:T(128)} %convert_element_type.15, () %tuple.17, (bf16[2048,2048]{1,0:T(8,128)(2,1)}, bf16[2048,6288]{0,1:T(8,128)(2,1)}, s32[]{:T(128)}, s32[8192]{0:T(1024)}, s32[]{:T(128)}) %tuple.18), branch_computations={%region_4.5_spmd, %region_5.10_spmd} | conditional | flops 52850606080 | bytes 137297984 | solution.py:49
  96.9 0.8 dynamic-slice_subtract_fusion
  97.7 63.0 %fusion.14 = (f32[2048]{0:T(1024)S(1)}, f32[2048,6288]{0,1:T(8,128)}) fusion(bf16[2048,2048]{1,0:T(8,128)(2,1)} %get-tuple-element.43, bf16[2048,6288]{0,1:T(8,128)(2,1)} %get-tuple-element.70), kind=kOutput, calls=%fused_computation.49 | convolution fusion | flops 52760444928 | bytes 85663744 | tf_op jit(solution)/shard_map/cond/branch_1_fun/dot_general | solution.py:20
  160.7 23.9 %fusion = (f32[2048]{0:T(1024)S(1)}, f32[2048]{0:T(1024)S(1)}, f32[2048]{0:T(1024)S(1)}) fusion(f32[2048,6288]{0,1:T(8,128)} %get-tuple-element.83, f32[2048]{0:T(1024)S(1)} %get-tuple-element.82, s32[2048]{0:T(1024)S(1)} %dynamic-slice_subtract_fusion), kind=kLoop, calls=%fused_computation.6 | loop fusion | flops 90138624 | bytes 51552256 | tf_op jit(solution)/shard_map/cond/branch_1_fun/reduce_sum | solution.py:23
  184.7 14.3 %pmax.7 = f32[2048]{0:T(1024)S(1)} all-reduce(f32[2048]{0:T(1024)S(1)} %bitcast.16), channel_id=1, replica_groups=mesh['tok'=4,'voc'=8] {'voc'}, use_global_device_ids=true, to_apply=%region_11.12 | all-reduce | flops 2048 | bytes 16384 | tf_op jit(solution)/shard_map/pmax | solution.py:76
  199.0 26.0 %all-reduce = (f32[2048]{0:T(1024)S(1)}, f32[2048]{0:T(1024)S(1)}, f32[2048]{0:T(1024)S(1)}) all-reduce(f32[2048]{0:T(1024)S(1)} %bitcast.22, f32[2048]{0:T(1024)S(1)} %get-tuple-element.91, f32[2048]{0:T(1024)S(1)} %get-tuple-element.90), channel_id=1, replica_groups=mesh['tok'=4,'voc'=8] {'voc'}, use_global_device_ids=true, to_apply=%region_10.11 | all-reduce | flops 6144 | bytes 49152 | tf_op jit(solution)/shard_map/psum | solution.py:78
  225.0 8.3 %all_gather.11 = f32[8192]{0:T(1024)S(1)} all-gather(f32[2048]{0:T(1024)S(1)} %get-tuple-element.88), channel_id=1, replica_groups=mesh['tok'=4,'voc'=8] {'tok'}, dimensions={0}, use_global_device_ids=true | all-gather | bytes 40960 | tf_op jit(solution)/shard_map/all_gather | solution.py:82
  233.3 8.1 %all_gather.10 = f32[8192]{0:T(1024)S(1)} all-gather(f32[2048]{0:T(1024)S(1)} %get-tuple-element.89), channel_id=1, replica_groups=mesh['tok'=4,'voc'=8] {'tok'}, dimensions={0}, use_global_device_ids=true | all-gather | bytes 40960 | tf_op jit(solution)/shard_map/all_gather | solution.py:81
  241.5 2.0 gather_fusion.1
  243.5 2.0 gather_fusion
  (11 shorter events, 0.1 us)
Async XLA Ops:
  7.2 89.7 %all-gather.2.cloned.1.call-start = ((), (), s32[]{:S(2)}) async-start(), calls=%async_computation | async-start | bytes 9437184 | tf_op jit(solution)/shard_map/all_gather | solution.py:75
Sparse Core Ops, SparseCore 0:
  12.1 84.7 all-gather.1
where the time goes:
time: 253 us; the launch traced here: 252 us
  waiting for transfers between devices  80.3 us (32%)
  matrix products  63 us (25%)
  blocking collectives  56.7 us (22%)
  other arithmetic  33.5 us (13%)
  between operations  14.8 us (6%)
  local copies, waits for them, and re-layouts  4.07 us (2%)
    all_gather x1, waiting for transfers between devices, on_device(): lax.all_gather(normed, 'voc', axis=0, tiled=True)  80.3 us
    dot_general x1, matrix products, row_stats(): logits = jnp.dot(piece, weights, preferred_element_type=jnp.float32)  63 us
    psum x1, blocking collectives, on_device(): lax.psum((stats[1] * factor, stats[2] * factor, stats[3]), 'voc')  26 us
    reduce_sum x1, other arithmetic, row_stats(): total = jnp.sum(expo, axis=1)  23.9 us
    pmax x1, blocking collectives, on_device(): top = lax.pmax(stats[0], 'voc')  14.3 us
    all_gather x1, blocking collectives, on_device(): lax.all_gather(own_ent, 'tok', axis=0, tiled=True)  8.35 us
    all_gather x1, blocking collectives, on_device(): lax.all_gather(own_lp, 'tok', axis=0, tiled=True)  8.14 us
  transfers between devices with their start and end apart: 1, of which 1 were waited for; matrix products, arithmetic and copies ran while one was open for 2% of the time, Pallas kernels for 0%

commit v1 on v0

--- a/solution.py
+++ b/solution.py
@@ -4,6 +4,19 @@
 from jax.sharding import PartitionSpec as P
 
 MAXLEN = 1024
+
+
+def gather_around(x, axis, dim):
+    size, index, rows = (lax.axis_size(axis), lax.axis_index(axis), x.shape[dim])
+    forward = [(i, (i + 1) % size) for i in range(size)]
+    whole = jnp.zeros((*x.shape[:dim], size * rows, *x.shape[dim + 1 :]), x.dtype)
+    carried = x
+    for step in range(size):
+        holder = (index - step) % size
+        whole = lax.dynamic_update_slice_in_dim(whole, carried, holder * rows, axis=dim)
+        if step < size - 1:
+            carried = lax.ppermute(carried, axis, forward)
+    return whole
 
 
 def slot_rows(positions, lengths, perm):
@@ -72,7 +85,7 @@
     device = lax.axis_index(("tok", "voc"))
     group_rows = normed.shape[0] * n_voc
     compute = make_stats(head, voc_index * shard_cols, tok_index * group_rows, targets, slot_len)
-    stats = compute(lax.all_gather(normed, "voc", axis=0, tiled=True), jnp.int32(0))
+    stats = compute(gather_around(normed, "voc", 0), jnp.int32(0))
     top = lax.pmax(stats[0], "voc")
     factor = jnp.exp(stats[0] - top)
     total, moment, picked = lax.psum((stats[1] * factor, stats[2] * factor, stats[3]), "voc")

time: 253 us -> 289 us (1.14)
  waiting for transfers between devices: 80.3 us -> 109 us
  local copies, waits for them, and re-layouts: 4.07 us -> 25.2 us
  between operations: 14.8 us -> 1.37 us
    ppermute x0 -> x7, waiting for transfers between devices: none -> 109 us  [gather_around(): carried = lax.ppermute(carried, axis, forward)]
    all_gather x1 -> x0, waiting for transfers between devices: 80.3 us -> none  [on_device(): lax.all_gather(normed, 'voc', axis=0, tiled=True)]
    dynamic_update_slice x0 -> x8, local copies, waits for them, and re-layouts: none -> 14.8 us  [gather_around(): lax.dynamic_update_slice_in_dim(whole, carried, holder * rows, axis=dim)]
    broadcast_in_dim x0 -> x1, local copies, waits for them, and re-layouts: none -> 4.33 us  [gather_around(): jnp.zeros((*x.shape[:dim], size * rows, *x.shape[dim + 1:]), x.dtype)]
  transfers between devices with their start and end apart: 1 -> 7, of which waited for: 1 -> 7; matrix products, arithmetic and copies ran while one was open for 2% -> 1% of each run, Pallas kernels for 0% -> 0%
where the time goes in v1:
time: 289 us; the launch traced here: 288 us
  waiting for transfers between devices  109 us (38%)
  matrix products  63 us (22%)
  blocking collectives  56.8 us (20%)
  other arithmetic  32.5 us (11%)
  local copies, waits for them, and re-layouts  25.2 us (9%)
    ppermute x7, waiting for transfers between devices, gather_around(): carried = lax.ppermute(carried, axis, forward)  109 us
    dot_general x1, matrix products, row_stats(): logits = jnp.dot(piece, weights, preferred_element_type=jnp.float32)  63 us
    psum x1, blocking collectives, on_device(): lax.psum((stats[1] * factor, stats[2] * factor, stats[3]), 'voc')  26 us
    reduce_sum x1, other arithmetic, row_stats(): total = jnp.sum(expo, axis=1)  23.9 us
    dynamic_update_slice x8, local copies, waits for them, and re-layouts, gather_around(): lax.dynamic_update_slice_in_dim(whole, carried, holder * rows, axis=dim)  14.8 us
    pmax x1, blocking collectives, on_device(): top = lax.pmax(stats[0], 'voc')  13.9 us
    all_gather x1, blocking collectives, on_device(): lax.all_gather(own_ent, 'tok', axis=0, tiled=True)  8.7 us
    all_gather x1, blocking collectives, on_device(): lax.all_gather(own_lp, 'tok', axis=0, tiled=True)  8.14 us
  transfers between devices with their start and end apart: 7, of which 7 were waited for; matrix products, arithmetic and copies ran while one was open for 1% of the time, Pallas kernels for 0%

profile of v1, /device:TPU:0, one launch (start us, length us, event | category | flops | bytes accessed | tf_op | source)
XLA Modules:
  0.0 288.0 jit_solution(8080529540815183015)
XLA Ops:
  1.3 1.5 fusion.1
  2.8 1.5 fusion.3
  4.9 16.5 %collective-permute-done = bf16[256,2048]{1,0:T(8,128)(2,1)S(1)} collective-permute-done((bf16[256,2048]{1,0:T(8,128)(2,1)S(1)}, bf16[256,2048]{1,0:T(8,128)(2,1)S(1)}, u32[]{:S(2)}, u32[]{:S(2)}) %collective-permute-start) | collective-permute-done | bytes 1048608 | tf_op jit(solution)/shard_map/ppermute | solution.py:18
  21.4 16.0 %collective-permute-done.1 = bf16[256,2048]{1,0:T(8,128)(2,1)S(1)} collective-permute-done((bf16[256,2048]{1,0:T(8,128)(2,1)S(1)}, bf16[256,2048]{1,0:T(8,128)(2,1)S(1)}, u32[]{:S(2)}, u32[]{:S(2)}) %collective-permute-start.1) | collective-permute-done | bytes 1048608 | tf_op jit(solution)/shard_map/ppermute | solution.py:18
  37.5 16.0 %collective-permute-done.2 = bf16[256,2048]{1,0:T(8,128)(2,1)S(1)} collective-permute-done((bf16[256,2048]{1,0:T(8,128)(2,1)S(1)}, bf16[256,2048]{1,0:T(8,128)(2,1)S(1)}, u32[]{:S(2)}, u32[]{:S(2)}) %collective-permute-start.2) | collective-permute-done | bytes 1048608 | tf_op jit(solution)/shard_map/ppermute | solution.py:18
  54.5 16.0 %collective-permute-done.3 = bf16[256,2048]{1,0:T(8,128)(2,1)S(1)} collective-permute-done((bf16[256,2048]{1,0:T(8,128)(2,1)S(1)}, bf16[256,2048]{1,0:T(8,128)(2,1)S(1)}, u32[]{:S(2)}, u32[]{:S(2)}) %collective-permute-start.3) | collective-permute-done | bytes 1048608 | tf_op jit(solution)/shard_map/ppermute | solution.py:18
  71.5 16.1 %collective-permute-done.4 = bf16[256,2048]{1,0:T(8,128)(2,1)} collective-permute-done((bf16[256,2048]{1,0:T(8,128)(2,1)S(1)}, bf16[256,2048]{1,0:T(8,128)(2,1)}, u32[]{:S(2)}, u32[]{:S(2)}) %collective-permute-start.4) | collective-permute-done | bytes 1048608 | tf_op jit(solution)/shard_map/ppermute | solution.py:18
  90.7 13.2 %collective-permute-done.5 = bf16[256,2048]{1,0:T(8,128)(2,1)} collective-permute-done((bf16[256,2048]{1,0:T(8,128)(2,1)}, bf16[256,2048]{1,0:T(8,128)(2,1)}, u32[]{:S(2)}, u32[]{:S(2)}) %collective-permute-start.5) | collective-permute-done | bytes 1048608 | tf_op jit(solution)/shard_map/ppermute | solution.py:18
  105.5 14.8 %collective-permute-done.6 = bf16[256,2048]{1,0:T(8,128)(2,1)} collective-permute-done((bf16[256,2048]{1,0:T(8,128)(2,1)}, bf16[256,2048]{1,0:T(8,128)(2,1)}, u32[]{:S(2)}, u32[]{:S(2)}) %collective-permute-start.6) | collective-permute-done | bytes 1048608 | tf_op jit(solution)/shard_map/ppermute | solution.py:18
  120.3 106.9 %conditional.1 = (f32[4,2048]{1,0:T(4,128)S(1)}) conditional(s32[]{:T(128)} %convert_element_type.15, () %tuple.43, (pred[]{:T(512)}, bf16[256,2048]{1,0:T(8,128)(2,1)S(1)}, pred[]{:T(512)}, bf16[256,2048]{1,0:T(8,128)(2,1)S(1)}, pred[]{:T(512)}, /*index=5*/bf16[256,2048]{1,0:T(8,128)(2,1)S(1)}, pred[]{:T(512)}, ...), branch_computations={%region_4.5_spmd, %region_5.10_spmd.clone.clone} | conditional | flops 52850606080 | bytes 162464736 | solution.py:62
  120.3 4.3 %broadcast_in_dim.82 = bf16[2048,2048]{1,0:T(8,128)(2,1)} broadcast(bf16[]{:T(256)} %constant.129.clone.2), dimensions={} | broadcast | bytes 8388610 | tf_op jit(solution)/shard_map/broadcast_in_dim | solution.py:12
  127.8 2.3 constant_dynamic-update-slice_fusion.4
  130.2 2.3 constant_dynamic-update-slice_fusion.3
  132.4 2.3 constant_dynamic-update-slice_fusion.2
  134.7 2.4 constant_dynamic-update-slice_fusion.1
  137.1 2.3 constant_dynamic-update-slice_fusion
  139.4 63.0 %fusion.14 = (f32[2048]{0:T(1024)S(1)}, f32[2048,6288]{0,1:T(8,128)}) fusion(bf16[2048,2048]{1,0:T(8,128)(2,1)} %constant_dynamic-update-slice_fusion, bf16[2048,6288]{0,1:T(8,128)(2,1)} %get-tuple-element.715), kind=kOutput, calls=%fused_computation.57 | convolution fusion | flops 52760444928 | bytes 85663744 | tf_op jit(solution)/shard_map/cond/branch_1_fun/dot_general | solution.py:33
  203.2 23.9 %fusion = (f32[2048]{0:T(1024)S(1)}, f32[2048]{0:T(1024)S(1)}, f32[2048]{0:T(1024)S(1)}) fusion(f32[2048,6288]{0,1:T(8,128)} %get-tuple-element.792, f32[2048]{0:T(1024)S(1)} %get-tuple-element.791, s32[2048]{0:T(1024)S(1)} %dynamic-slice_subtract_fusion), kind=kLoop, calls=%fused_computation.6 | loop fusion | flops 90138624 | bytes 51552256 | tf_op jit(solution)/shard_map/cond/branch_1_fun/reduce_sum | solution.py:36
  227.2 13.9 %pmax.7 = f32[2048]{0:T(1024)S(1)} all-reduce(f32[2048]{0:T(1024)S(1)} %bitcast.20), channel_id=1, replica_groups=mesh['tok'=4,'voc'=8] {'voc'}, use_global_device_ids=true, to_apply=%region_11.12 | all-reduce | flops 2048 | bytes 16384 | tf_op jit(solution)/shard_map/pmax | solution.py:89
  241.2 26.0 %all-reduce = (f32[2048]{0:T(1024)S(1)}, f32[2048]{0:T(1024)S(1)}, f32[2048]{0:T(1024)S(1)}) all-reduce(f32[2048]{0:T(1024)S(1)} %bitcast.26, f32[2048]{0:T(1024)S(1)} %get-tuple-element.800, f32[2048]{0:T(1024)S(1)} %get-tuple-element.799), channel_id=1, replica_groups=mesh['tok'=4,'voc'=8] {'voc'}, use_global_device_ids=true, to_apply=%region_10.11 | all-reduce | flops 6144 | bytes 49152 | tf_op jit(solution)/shard_map/psum | solution.py:91
  267.1 8.7 %all_gather.7 = f32[8192]{0:T(1024)S(1)} all-gather(f32[2048]{0:T(1024)S(1)} %get-tuple-element.797), channel_id=1, replica_groups=mesh['tok'=4,'voc'=8] {'tok'}, dimensions={0}, use_global_device_ids=true | all-gather | bytes 40960 | tf_op jit(solution)/shard_map/all_gather | solution.py:95
  275.9 8.1 %all_gather.6 = f32[8192]{0:T(1024)S(1)} all-gather(f32[2048]{0:T(1024)S(1)} %get-tuple-element.798), channel_id=1, replica_groups=mesh['tok'=4,'voc'=8] {'tok'}, dimensions={0}, use_global_device_ids=true | all-gather | bytes 40960 | tf_op jit(solution)/shard_map/all_gather | solution.py:94
  284.0 2.0 gather_fusion.1
  286.0 2.0 gather_fusion
  (34 shorter events, 11.3 us)
Async XLA Ops:
  4.4 17.1 %collective-permute-start = (bf16[256,2048]{1,0:T(8,128)(2,1)S(1)}, bf16[256,2048]{1,0:T(8,128)(2,1)S(1)}, u32[]{:S(2)}, u32[]{:S(2)}) collective-permute-start(bf16[256,2048]{1,0:T(8,128)(2,1)S(1)} %fusion.3), channel_id=1, source_target_pairs={{0,1},{1,2},{2,3},{3,4},{4,5},{5,6},{6,7},{7,0},{8,9},{9,10},{10,1... | collective-permute-start | bytes 3145736 | tf_op jit(solution)/shard_map/ppermute | solution.py:18
  21.4 16.0 %collective-permute-start.1 = (bf16[256,2048]{1,0:T(8,128)(2,1)S(1)}, bf16[256,2048]{1,0:T(8,128)(2,1)S(1)}, u32[]{:S(2)}, u32[]{:S(2)}) collective-permute-start(bf16[256,2048]{1,0:T(8,128)(2,1)S(1)} %collective-permute-done), channel_id=1, source_target_pairs={{0,1},{1,2},{2,3},{3,4},{4,5},{5,6},{6,7},{7,0},{8,9},{9,10},{10,1... | collective-permute-start | bytes 3145736 | tf_op jit(solution)/shard_map/ppermute | solution.py:18
  37.5 16.0 %collective-permute-start.2 = (bf16[256,2048]{1,0:T(8,128)(2,1)S(1)}, bf16[256,2048]{1,0:T(8,128)(2,1)S(1)}, u32[]{:S(2)}, u32[]{:S(2)}) collective-permute-start(bf16[256,2048]{1,0:T(8,128)(2,1)S(1)} %collective-permute-done.1), channel_id=1, source_target_pairs={{0,1},{1,2},{2,3},{3,4},{4,5},{5,6},{6,7},{7,0},{8,9},{9,10},{10,1... | collective-permute-start | bytes 3145736 | tf_op jit(solution)/shard_map/ppermute | solution.py:18
  53.5 1.0 copy-start
  54.5 16.0 %collective-permute-start.3 = (bf16[256,2048]{1,0:T(8,128)(2,1)S(1)}, bf16[256,2048]{1,0:T(8,128)(2,1)S(1)}, u32[]{:S(2)}, u32[]{:S(2)}) collective-permute-start(bf16[256,2048]{1,0:T(8,128)(2,1)S(1)} %collective-permute-done.2), channel_id=1, source_target_pairs={{0,1},{1,2},{2,3},{3,4},{4,5},{5,6},{6,7},{7,0},{8,9},{9,10},{10,1... | collective-permute-start | bytes 3145736 | tf_op jit(solution)/shard_map/ppermute | solution.py:18
  70.5 1.0 copy-start.1
  71.5 16.1 %collective-permute-start.4 = (bf16[256,2048]{1,0:T(8,128)(2,1)S(1)}, bf16[256,2048]{1,0:T(8,128)(2,1)}, u32[]{:S(2)}, u32[]{:S(2)}) collective-permute-start(bf16[256,2048]{1,0:T(8,128)(2,1)S(1)} %collective-permute-done.3), channel_id=1, source_target_pairs={{0,1},{1,2},{2,3},{3,4},{4,5},{5,6},{6,7},{7,0},{8,9},{9,10},{10,1... | collective-permute-start | bytes 3145736 | tf_op jit(solution)/shard_map/ppermute | solution.py:18
  87.6 16.3 %collective-permute-start.5 = (bf16[256,2048]{1,0:T(8,128)(2,1)}, bf16[256,2048]{1,0:T(8,128)(2,1)}, u32[]{:S(2)}, u32[]{:S(2)}) collective-permute-start(bf16[256,2048]{1,0:T(8,128)(2,1)} %collective-permute-done.4), channel_id=1, source_target_pairs={{0,1},{1,2},{2,3},{3,4},{4,5},{5,6},{6,7},{7,0},{8,9},{9,10},{10,1... | collective-permute-start | bytes 3145736 | tf_op jit(solution)/shard_map/ppermute | solution.py:18
  104.0 16.3 %collective-permute-start.6 = (bf16[256,2048]{1,0:T(8,128)(2,1)}, bf16[256,2048]{1,0:T(8,128)(2,1)}, u32[]{:S(2)}, u32[]{:S(2)}) collective-permute-start(bf16[256,2048]{1,0:T(8,128)(2,1)} %collective-permute-done.5), channel_id=1, source_target_pairs={{0,1},{1,2},{2,3},{3,4},{4,5},{5,6},{6,7},{7,0},{8,9},{9,10},{10,1... | collective-permute-start | bytes 3145736 | tf_op jit(solution)/shard_map/ppermute | solution.py:18
